TPU v7x, 256 devices: a whole 4x4x8 slice. The times are simulated.
256 devices in a mesh: stn: 64 (over y, z, core), sec: 4 (over x).
Axes of the slice: x: 4, y: 4, z: 8, core: 2. Of those that a mesh axis runs over, the one named last changes fastest.
Arguments:
- voltages: bfloat16 [2, 1024, 569344], P(None, ('stn', 'sec')), may hold values from -6 to 6
- fir_taps: float32 [12, 4096], replicated, may hold values from -1.75 to 1.75
- cor_channels: int32 [256], replicated, may hold values from 0 to 4095, as said below
- beam_channels: int32 [256], replicated, may hold values from 1 to 4094, as said below
- cor_gain: float32 [256], replicated, as said below
- beam_gain: float32 [256], replicated, as said below
- beam_stations: int32 [16, 512], replicated, may hold values from 0 to 511
- beam_codes: int32 [16, 512], replicated, may hold values from 0 to 255
Outputs:
- visibilities: bfloat16 [256, 2, 1024, 1024], P(('stn', 'sec'))
- beams: bfloat16 [256, 16, 2, 256], P(('stn', 'sec'))
Inputs may be any that keep to these rules, and one draw needn't show every extreme that they name: cor_channels and beam_channels together are 512 distinct transform channels. None of beam_channels appears in cor_channels. `cor_gain`: positive. `beam_gain`: positive.
All inputs are finite; a program needn't handle non-finite values.
Results may differ from a plain program's by a relative error of at most 0.0085.
Values may be sent and summed in bfloat16 or wider, within the bound.
No kernel may reach another device: no remote copies, remote signals or barrier semaphores. Data moves between devices by JAX's collectives and lax.ppermute only.
A program may use at most 128 MiB of HBM per device.

v0:
```python
import math
import jax
import jax.numpy as jnp
from jax import lax
from jax.sharding import PartitionSpec as P

STATIONS = 512
epsilon = 1e-05


def make_tables(channel_of, points):
    sample_index = jnp.arange(points, dtype=jnp.int32)
    phase_turns = channel_of[:, None] * sample_index[None, :] % points
    phase_angle = phase_turns.astype(jnp.float32) * (2.0 * math.pi / points)
    table_scale = 1.0 / math.sqrt(points)
    cos_table = (jnp.cos(phase_angle) * table_scale).astype(jnp.bfloat16)
    sin_table = (jnp.sin(phase_angle) * table_scale).astype(jnp.bfloat16)
    return (cos_table, sin_table)


def make_weights(beam_stations, beam_codes, stations):
    station_ids = jnp.arange(stations, dtype=jnp.int32)
    onehot = (beam_stations[:, :, None] == station_ids[None, None, :]).astype(jnp.float32)
    amplitude = (1 + beam_codes // 64).astype(jnp.float32)
    phase_angle = (beam_codes % 64).astype(jnp.float32) * (2.0 * math.pi / 64.0)
    weight_re = jnp.einsum("bk,bks->bs", amplitude * jnp.cos(phase_angle), onehot)
    weight_im = jnp.einsum("bk,bks->bs", amplitude * jnp.sin(phase_angle), onehot)
    return (weight_re.astype(jnp.bfloat16), weight_im.astype(jnp.bfloat16))


def polyphase(in_block, fir_taps, spectra):
    tap_count, points = fir_taps.shape
    framed = in_block.reshape(in_block.shape[0], in_block.shape[1], -1, points)
    summed = jnp.zeros((framed.shape[0], framed.shape[1], spectra, points), jnp.float32)
    for tap_index in range(tap_count):
        summed = summed + fir_taps[tap_index] * framed[
            :, :, tap_index : tap_index + spectra, :
        ].astype(jnp.float32)
    return summed.astype(jnp.bfloat16)


def contract(left_rows, right_rows):
    contract_dims = (((1,), (1,)), ((), ()))
    return lax.dot_general(left_rows, right_rows, contract_dims, preferred_element_type=jnp.float32)


def spectrum(filtered, cos_table, sin_table, slot_gain):
    inputs_here, spectra, points = (filtered.shape[1], filtered.shape[2], filtered.shape[3])
    real_rows = filtered[0].reshape(inputs_here * spectra, points)
    imag_rows = filtered[1].reshape(inputs_here * spectra, points)
    spec_re = contract(cos_table, real_rows) + contract(sin_table, imag_rows)
    spec_im = contract(cos_table, imag_rows) - contract(sin_table, real_rows)
    combined = jnp.concatenate(
        [spec_re.reshape(-1, inputs_here, spectra), spec_im.reshape(-1, inputs_here, spectra)],
        axis=2,
    )
    return (combined * slot_gain[:, None, None]).astype(jnp.bfloat16)


def form_beams(beam_data, weight_re, weight_im):
    spectra = beam_data.shape[2] // 2
    samples = beam_data.reshape(beam_data.shape[0], -1, 2, beam_data.shape[2])
    with_re = jnp.einsum("bs,jspt->jbpt", weight_re, samples, preferred_element_type=jnp.float32)
    with_im = jnp.einsum("bs,jspt->jbpt", weight_im, samples, preferred_element_type=jnp.float32)
    out_re = with_re[..., :spectra] - with_im[..., spectra:]
    out_im = with_re[..., spectra:] + with_im[..., :spectra]
    return jnp.concatenate([out_re, out_im], axis=3)


def per_device(
    voltages, fir_taps, cor_channels, beam_channels, cor_gain, beam_gain, beam_stations, beam_codes
):
    tap_count, points = fir_taps.shape
    stn_count = lax.axis_size("stn")
    sec_count = lax.axis_size("sec")
    device_count = stn_count * sec_count
    inputs_here = voltages.shape[1]
    spectra = voltages.shape[2] // points - tap_count + 1
    filtered = polyphase(voltages, fir_taps, spectra)
    channel_of = jnp.concatenate([cor_channels, beam_channels])
    slot_gain = jnp.concatenate([cor_gain, beam_gain])
    cos_table, sin_table = make_tables(channel_of, points)
    weight_re, weight_im = make_weights(beam_stations, beam_codes, STATIONS)
    spectra_all = spectrum(filtered, cos_table, sin_table, slot_gain)
    outgoing = spectra_all.reshape(2, stn_count, sec_count, 1, 1, inputs_here, 2 * spectra)
    turned = lax.all_to_all(
        lax.all_to_all(outgoing, "stn", split_axis=1, concat_axis=3, tiled=True),
        "sec",
        split_axis=2,
        concat_axis=4,
        tiled=True,
    )
    received = turned.reshape(2, device_count * inputs_here, 2 * spectra)
    cor_data = received[0]
    beam_data = received[1:2]
    swapped = jnp.concatenate([cor_data[:, spectra:], -cor_data[:, :spectra]], axis=1)
    vis_re = contract(cor_data, cor_data) / spectra
    vis_im = contract(swapped, cor_data) / spectra
    visibilities = jnp.stack([vis_re, vis_im])[None].astype(jnp.bfloat16)
    raw_beams = form_beams(beam_data, weight_re, weight_im)
    local_power = jnp.sum(raw_beams * raw_beams, axis=(0, 2, 3))
    summed_power = lax.psum(local_power, ("stn", "sec"))
    beam_power = summed_power / (device_count * raw_beams.shape[2] * raw_beams.shape[3])
    beams = (raw_beams * lax.rsqrt(beam_power + epsilon)[None, :, None, None]).astype(jnp.bfloat16)
    return (visibilities, beams)


def solution(mesh):
    in_specs = (P(None, ("stn", "sec"), None), P(), P(), P(), P(), P(), P(), P())
    out_specs = (P(("stn", "sec"), None, None, None), P(("stn", "sec"), None, None, None))
    return jax.shard_map(
        per_device, mesh=mesh, in_specs=in_specs, out_specs=out_specs, check_vma=False
    )
```

profile of v0, /device:TPU:1, one launch (start us, length us, event | category | flops | bytes accessed | tf_op | source)
XLA Modules:
  0.0 348.5 jit_solution(4968068274849040461)
XLA Ops:
  0.6 1.8 fusion.60
  2.5 14.5 %reshape.175 = bf16[2,4,139,4096]{3,2,1,0:T(8,128)(2,1)} reshape(bf16[2,4,569344]{2,1,0:T(4,128)(2,1)} %param.8) | data formatting | bytes 18219008 | tf_op jit(solution)/shard_map/reshape | solution.py:33
  17.0 52.5 %add_convert_fusion = bf16[2,4,128,4096]{3,2,1,0:T(8,128)(2,1)} fusion(bf16[2,4,139,4096]{3,2,1,0:T(8,128)(2,1)} %reshape.175, f32[4096]{0:T(1024)S(1)} %bitcast.81, f32[4096]{0:T(1024)S(1)} %bitcast.82, f32[4096]{0:T(1024)S(1)} %bitcast.72, f32[4096]{0:T(1024)S(1)} %bitcast.73, f32[4096]{0:T(1024)S(1)} %bitcast.74, f32[4096]{0:T(1024)S(1)} %bitcast.75, ...), kind=kLoop, calls=%fused_computation.3 | loop fusion | flops 150994944 | bytes 109248512 | tf_op jit(solution)/shard_map/convert_element_type | solution.py:39
  69.5 0.0 copy-start.5
  69.5 4.0 %fusion.57 = (bf16[1,4,128,4096]{3,2,1,0:T(8,128)(2,1)S(1)}, bf16[1,4,128,4096]{3,2,1,0:T(8,128)(2,1)S(1)}) fusion(bf16[2,4,128,4096]{3,2,1,0:T(8,128)(2,1)} %add_convert_fusion), kind=kLoop, calls=%fused_computation.88 | loop fusion | bytes 16777216 | tf_op jit(solution)/shard_map/slice | solution.py:49
  73.5 0.0 copy-done.4
  73.5 0.0 copy-done.5
  73.5 0.0 copy-start
  73.6 31.8 %fusion.11 = f32[512,512]{1,0:T(8,128)S(1)} fusion(bf16[512,4096]{1,0:T(8,128)(2,1)S(1)} %bitcast.67, s32[512]{0:T(512)S(1)} %pad_add_fusion), kind=kOutput, calls=%fused_computation.21 | convolution fusion | flops 2181038080 | bytes 5244928 | tf_op jit(solution)/shard_map/dot_general | solution.py:44
  105.4 0.0 copy-done
  105.4 32.4 %fusion.10 = f32[512,512]{1,0:T(8,128)} fusion(bf16[512,4096]{1,0:T(8,128)(2,1)S(1)} %bitcast.69, s32[512]{0:T(512)S(1)} %pad_add_fusion), kind=kOutput, calls=%fused_computation.20 | convolution fusion | flops 2181038080 | bytes 5244928 | tf_op jit(solution)/shard_map/dot_general | solution.py:44
  137.7 32.1 %fusion.17 = f32[512,512]{1,0:T(8,128)S(1)} fusion(f32[512,512]{1,0:T(8,128)S(1)} %fusion.11, bf16[512,4096]{1,0:T(8,128)(2,1)S(1)} %bitcast.70, s32[512]{0:T(512)S(1)} %pad_add_fusion), kind=kOutput, calls=%fused_computation.29 | convolution fusion | flops 2181300224 | bytes 6293504 | tf_op jit(solution)/shard_map/dot_general | solution.py:44
  169.8 0.4 concatenate.56
  170.2 0.0 copy-start.2
  170.2 0.0 copy-start.3
  170.2 34.4 %fusion.18 = f32[512,512]{1,0:T(8,128)S(1)} fusion(f32[512,512]{1,0:T(8,128)} %fusion.10, bf16[512,4096]{1,0:T(8,128)(2,1)} %bitcast.68, s32[512]{0:T(512)S(1)} %pad_add_fusion), kind=kOutput, calls=%fused_computation.30 | convolution fusion | flops 2181300224 | bytes 6293504 | tf_op jit(solution)/shard_map/dot_general | solution.py:44
  204.7 0.0 copy-start.1
  204.7 0.0 copy-start.6
  204.7 0.4 concatenate.57
  205.0 0.0 copy-done.2
  205.1 0.1 concatenate.59
  205.2 0.0 copy-done.3
  205.2 0.1 concatenate.60
  205.3 0.1 copy.37
  205.4 0.7 fusion.14
  206.1 41.5 %all_to_all.33 = bf16[2,64,4,1,1,4,256]{6,5,2,0,4,3,1:T(4,128)(2,1)S(1)} all-to-all(bf16[2,64,4,1,1,4,256]{6,5,2,0,4,3,1:T(4,128)(2,1)S(1)} %fusion.14), channel_id=1, replica_groups=mesh['stn'=64,'sec'=4] {'stn'}, dimensions={1} | all-to-all | bytes 2097152 | tf_op jit(solution)/shard_map/all_to_all | solution.py:87
  247.6 1.4 copy.38
  249.0 4.0 %all-to-all-start.1 = ((bf16[2,1,4,64,1,4,256]{6,5,3,0,4,1,2:T(4,128)(2,1)}), bf16[2,1,4,64,1,4,256]{6,5,3,0,4,1,2:T(4,128)(2,1)S(1)}, u32[]{:S(2)}, u32[]{:S(2)}) async-start(bf16[2,1,4,64,1,4,256]{6,5,3,0,4,1,2:T(4,128)(2,1)} %copy.38), calls=%async_computation.1 | async-start | bytes 2097152 | tf_op jit(solution)/shard_map/all_to_all | solution.py:86
  253.0 0.0 copy-done.1
  253.0 0.2 multiply_bitcast_fusion.1
  253.2 3.2 fusion
  256.4 3.2 fusion.1
  259.6 8.3 %all-to-all-done.1 = bf16[2,1,4,64,1,4,256]{6,5,3,0,4,1,2:T(4,128)(2,1)S(1)} async-done(((bf16[2,1,4,64,1,4,256]{6,5,3,0,4,1,2:T(4,128)(2,1)}), bf16[2,1,4,64,1,4,256]{6,5,3,0,4,1,2:T(4,128)(2,1)S(1)}, u32[]{:S(2)}, u32[]{:S(2)}) %all-to-all-start.1) | async-done | bytes 1048608 | tf_op jit(solution)/shard_map/all_to_all | solution.py:86
  267.9 0.4 fusion.58
  268.3 0.2 copy.40
  268.5 0.3 reshape.176
  268.7 0.2 convolution_bitcast_fusion
  268.9 0.2 convolution_bitcast_fusion.1
  269.1 0.2 copy.39
  269.3 0.1 squeeze.3
  269.4 0.1 fusion.59
  269.5 0.1 multiply_reduce_fusion
  269.6 0.7 fusion.15
  270.4 74.1 %psum.7 = f32[16]{0:T(128)S(1)} all-reduce(f32[16]{0:T(128)S(1)} %multiply_reduce_fusion), channel_id=1, replica_groups=mesh['stn'=64,'sec'=4] {'stn','sec'}, use_global_device_ids=true, to_apply=%region_1.2 | all-reduce | flops 16 | bytes 128 | tf_op jit(solution)/shard_map/psum | solution.py:102
  344.4 0.1 multiply_convert_fusion.12
  344.5 0.6 copy.43
  345.1 0.7 fusion.16
  345.9 2.4 pad_maximum_fusion
  (6 shorter events, 0.0 us)
Async XLA Ops:
  69.5 4.0 %copy-start.4 = (s32[256]{0:T(256)S(1)}, s32[256]{0:T(256)}, u32[]{:S(2)}) copy-start(s32[256]{0:T(256)} %param.11) | copy-start | bytes 3076
  69.5 4.0 %copy-start.5 = (s32[256]{0:T(256)S(1)}, s32[256]{0:T(256)}, u32[]{:S(2)}) copy-start(s32[256]{0:T(256)} %param.10) | copy-start | bytes 3076
  73.5 31.8 %copy-start = (bf16[1,4,128,4096]{3,2,1,0:T(8,128)(2,1)}, bf16[1,4,128,4096]{3,2,1,0:T(8,128)(2,1)S(1)}, u32[]{:S(2)}) copy-start(bf16[1,4,128,4096]{3,2,1,0:T(8,128)(2,1)S(1)} %get-tuple-element.12) | copy-start | bytes 12582916
  170.2 34.8 %copy-start.2 = (f32[256]{0:T(256)S(1)}, f32[256]{0:T(256)}, u32[]{:S(2)}) copy-start(f32[256]{0:T(256)} %param.12) | copy-start | bytes 3076
  170.2 35.0 %copy-start.3 = (f32[256]{0:T(256)S(1)}, f32[256]{0:T(256)}, u32[]{:S(2)}) copy-start(f32[256]{0:T(256)} %param.13) | copy-start | bytes 3076
  204.7 48.4 %copy-start.1 = (s32[16,512]{1,0:T(8,128)S(1)}, s32[16,512]{1,0:T(8,128)}, u32[]{:S(2)}) copy-start(s32[16,512]{1,0:T(8,128)} %param.15) | copy-start | bytes 98308
  204.7 48.5 %copy-start.6 = (s32[16,512]{1,0:T(8,128)S(1)}, s32[16,512]{1,0:T(8,128)}, u32[]{:S(2)}) copy-start(s32[16,512]{1,0:T(8,128)} %param.14) | copy-start | bytes 98308
  249.0 18.9 %all-to-all-start.1 = ((bf16[2,1,4,64,1,4,256]{6,5,3,0,4,1,2:T(4,128)(2,1)}), bf16[2,1,4,64,1,4,256]{6,5,3,0,4,1,2:T(4,128)(2,1)S(1)}, u32[]{:S(2)}, u32[]{:S(2)}) async-start(bf16[2,1,4,64,1,4,256]{6,5,3,0,4,1,2:T(4,128)(2,1)} %copy.38), calls=%async_computation.1 | async-start | bytes 2097152 | tf_op jit(solution)/shard_map/all_to_all | solution.py:86
where the time goes:
time: 352 us; the launch traced here: 348 us
  matrix products  139 us (39%)
  blocking collectives  116 us (33%)
  other arithmetic  56.1 us (16%)
  local copies, waits for them, and re-layouts  24.4 us (7%)
  waiting for transfers between devices  8.26 us (2%)
  starting transfers between devices  4.03 us (1%)
    dot_general x6, matrix products, contract(): lax.dot_general(left_rows, right_rows, contract_dims, preferred_element_t...  132 us
    psum x1, blocking collectives, per_device(): summed_power = lax.psum(local_power, ('stn', 'sec'))  74.1 us
    convert_element_type x1, other arithmetic, polyphase(): return summed.astype(jnp.bfloat16)  52.5 us
    all_to_all x1, blocking collectives, per_device(): lax.all_to_all(outgoing, 'stn', split_axis=1, concat_axis=3, tiled=True)  41.5 us
    reshape x1, local copies, waits for them, and re-layouts, polyphase(): framed = in_block.reshape(in_block.shape[0], in_block.shape[1], -1, points)  14.5 us
    all_to_all x1, waiting for transfers between devices, per_device(): lax.all_to_all(lax.all_to_all(outgoing, 'stn', split_axis=1, concat_axis=...  8.26 us
  transfers between devices with their start and end apart: 1, of which 1 were waited for; matrix products, arithmetic and copies ran while one was open for 2% of the time, Pallas kernels for 0%

commit v1 on v0

--- a/solution.py
+++ b/solution.py
@@ -99,7 +99,9 @@
     visibilities = jnp.stack([vis_re, vis_im])[None].astype(jnp.bfloat16)
     raw_beams = form_beams(beam_data, weight_re, weight_im)
     local_power = jnp.sum(raw_beams * raw_beams, axis=(0, 2, 3))
-    summed_power = lax.psum(local_power, ("stn", "sec"))
+    summed_power = local_power
+    for axis in ("sec", "stn"):
+        summed_power = lax.psum(summed_power, axis)
     beam_power = summed_power / (device_count * raw_beams.shape[2] * raw_beams.shape[3])
     beams = (raw_beams * lax.rsqrt(beam_power + epsilon)[None, :, None, None]).astype(jnp.bfloat16)
     return (visibilities, beams)

time: 352 us -> 411 us (1.17)
  blocking collectives: 116 us -> 175 us
    psum x1 -> x2, blocking collectives: 74.1 us -> 133 us  [per_device(): summed_power = lax.psum(summed_power, axis)]
where the time goes in v1:
time: 411 us; the launch traced here: 408 us
  blocking collectives  175 us (43%)
  matrix products  139 us (34%)
  other arithmetic  56 us (14%)
  local copies, waits for them, and re-layouts  24.4 us (6%)
  waiting for transfers between devices  8.26 us (2%)
    psum x2, blocking collectives, per_device(): summed_power = lax.psum(summed_power, axis)  133 us
    dot_general x6, matrix products, contract(): lax.dot_general(left_rows, right_rows, contract_dims, preferred_element_t...  132 us
    convert_element_type x1, other arithmetic, polyphase(): return summed.astype(jnp.bfloat16)  52.4 us
    all_to_all x1, blocking collectives, per_device(): lax.all_to_all(outgoing, 'stn', split_axis=1, concat_axis=3, tiled=True)  41.5 us
    reshape x1, local copies, waits for them, and re-layouts, polyphase(): framed = in_block.reshape(in_block.shape[0], in_block.shape[1], -1, points)  14.5 us
    all_to_all x1, waiting for transfers between devices, per_device(): lax.all_to_all(lax.all_to_all(outgoing, 'stn', split_axis=1, concat_axis=...  8.26 us
  transfers between devices with their start and end apart: 1, of which 1 were waited for; matrix products, arithmetic and copies ran while one was open for 2% of the time, Pallas kernels for 0%

profile of v1, /device:TPU:1, one launch (start us, length us, event | category | flops | bytes accessed | tf_op | source)
XLA Modules:
  0.0 407.8 jit_solution(10272800225670803010)
XLA Ops:
  0.6 1.8 fusion.60
  2.5 14.5 %reshape.175 = bf16[2,4,139,4096]{3,2,1,0:T(8,128)(2,1)} reshape(bf16[2,4,569344]{2,1,0:T(4,128)(2,1)} %param.8) | data formatting | bytes 18219008 | tf_op jit(solution)/shard_map/reshape | solution.py:33
  17.0 52.4 %add_convert_fusion = bf16[2,4,128,4096]{3,2,1,0:T(8,128)(2,1)} fusion(bf16[2,4,139,4096]{3,2,1,0:T(8,128)(2,1)} %reshape.175, f32[4096]{0:T(1024)S(1)} %bitcast.81, f32[4096]{0:T(1024)S(1)} %bitcast.82, f32[4096]{0:T(1024)S(1)} %bitcast.72, f32[4096]{0:T(1024)S(1)} %bitcast.73, f32[4096]{0:T(1024)S(1)} %bitcast.74, f32[4096]{0:T(1024)S(1)} %bitcast.75, ...), kind=kLoop, calls=%fused_computation.3 | loop fusion | flops 150994944 | bytes 109248512 | tf_op jit(solution)/shard_map/convert_element_type | solution.py:39
  69.4 0.0 copy-start.5
  69.4 4.0 fusion.57
  73.4 0.0 copy-done.4
  73.4 0.0 copy-done.5
  73.4 0.0 copy-start
  73.4 31.8 %fusion.11 = f32[512,512]{1,0:T(8,128)S(1)} fusion(bf16[512,4096]{1,0:T(8,128)(2,1)S(1)} %bitcast.67, s32[512]{0:T(512)S(1)} %pad_add_fusion), kind=kOutput, calls=%fused_computation.21 | convolution fusion | flops 2181038080 | bytes 5244928 | tf_op jit(solution)/shard_map/dot_general | solution.py:44
  105.3 0.0 copy-done
  105.3 32.4 %fusion.10 = f32[512,512]{1,0:T(8,128)} fusion(bf16[512,4096]{1,0:T(8,128)(2,1)S(1)} %bitcast.69, s32[512]{0:T(512)S(1)} %pad_add_fusion), kind=kOutput, calls=%fused_computation.20 | convolution fusion | flops 2181038080 | bytes 5244928 | tf_op jit(solution)/shard_map/dot_general | solution.py:44
  137.6 32.1 %fusion.17 = f32[512,512]{1,0:T(8,128)S(1)} fusion(f32[512,512]{1,0:T(8,128)S(1)} %fusion.11, bf16[512,4096]{1,0:T(8,128)(2,1)S(1)} %bitcast.70, s32[512]{0:T(512)S(1)} %pad_add_fusion), kind=kOutput, calls=%fused_computation.29 | convolution fusion | flops 2181300224 | bytes 6293504 | tf_op jit(solution)/shard_map/dot_general | solution.py:44
  169.7 0.4 concatenate.56
  170.1 0.0 copy-start.2
  170.1 0.0 copy-start.3
  170.1 34.4 %fusion.18 = f32[512,512]{1,0:T(8,128)S(1)} fusion(f32[512,512]{1,0:T(8,128)} %fusion.10, bf16[512,4096]{1,0:T(8,128)(2,1)} %bitcast.68, s32[512]{0:T(512)S(1)} %pad_add_fusion), kind=kOutput, calls=%fused_computation.30 | convolution fusion | flops 2181300224 | bytes 6293504 | tf_op jit(solution)/shard_map/dot_general | solution.py:44
  204.5 0.0 copy-start.1
  204.6 0.0 copy-start.6
  204.6 0.4 concatenate.57
  204.9 0.0 copy-done.2
  205.0 0.1 concatenate.59
  205.1 0.0 copy-done.3
  205.1 0.1 concatenate.60
  205.2 0.1 copy.37
  205.3 0.7 fusion.14
  206.0 41.5 %all_to_all.33 = bf16[2,64,4,1,1,4,256]{6,5,2,0,4,3,1:T(4,128)(2,1)S(1)} all-to-all(bf16[2,64,4,1,1,4,256]{6,5,2,0,4,3,1:T(4,128)(2,1)S(1)} %fusion.14), channel_id=1, replica_groups=mesh['stn'=64,'sec'=4] {'stn'}, dimensions={1} | all-to-all | bytes 2097152 | tf_op jit(solution)/shard_map/all_to_all | solution.py:87
  247.5 1.4 copy.38
  248.9 4.0 all-to-all-start.1
  252.9 0.2 multiply_bitcast_fusion.1
  253.1 3.2 fusion
  256.3 3.2 fusion.1
  259.5 8.3 %all-to-all-done.1 = bf16[2,1,4,64,1,4,256]{6,5,3,0,4,1,2:T(4,128)(2,1)S(1)} async-done(((bf16[2,1,4,64,1,4,256]{6,5,3,0,4,1,2:T(4,128)(2,1)}), bf16[2,1,4,64,1,4,256]{6,5,3,0,4,1,2:T(4,128)(2,1)S(1)}, u32[]{:S(2)}, u32[]{:S(2)}) %all-to-all-start.1) | async-done | bytes 1048608 | tf_op jit(solution)/shard_map/all_to_all | solution.py:86
  267.8 0.4 fusion.58
  268.2 0.2 copy.40
  268.4 0.3 reshape.176
  268.6 0.2 convolution_bitcast_fusion
  268.8 0.2 convolution_bitcast_fusion.1
  269.0 0.1 multiply_reduce_fusion
  269.1 6.9 %psum.14 = f32[16]{0:T(128)S(1)} all-reduce(f32[16]{0:T(128)S(1)} %multiply_reduce_fusion), channel_id=1, replica_groups=mesh['stn'=64,'sec'=4] {'sec'}, use_global_device_ids=true, to_apply=%region_1.2 | all-reduce | flops 16 | bytes 128 | tf_op jit(solution)/shard_map/psum | solution.py:104
  276.0 0.2 copy.39
  276.2 0.1 squeeze.3
  276.4 0.1 fusion.59
  276.4 0.7 fusion.15
  277.2 126.6 %psum.15 = f32[16]{0:T(128)S(1)} all-reduce(f32[16]{0:T(128)S(1)} %psum.14), channel_id=1, replica_groups=mesh['stn'=64,'sec'=4] {'stn'}, use_global_device_ids=true, to_apply=%region_2.3 | all-reduce | flops 16 | bytes 128 | tf_op jit(solution)/shard_map/psum | solution.py:104
  403.7 0.1 multiply_convert_fusion.12
  403.8 0.6 copy.43
  404.5 0.7 fusion.16
  405.2 2.4 pad_maximum_fusion
  (7 shorter events, 0.0 us)
Async XLA Ops:
  69.4 4.0 copy-start.4
  69.4 4.0 copy-start.5
  73.4 31.8 %copy-start = (bf16[1,4,128,4096]{3,2,1,0:T(8,128)(2,1)}, bf16[1,4,128,4096]{3,2,1,0:T(8,128)(2,1)S(1)}, u32[]{:S(2)}) copy-start(bf16[1,4,128,4096]{3,2,1,0:T(8,128)(2,1)S(1)} %get-tuple-element.12) | copy-start | bytes 12582916
  170.1 34.8 %copy-start.2 = (f32[256]{0:T(256)S(1)}, f32[256]{0:T(256)}, u32[]{:S(2)}) copy-start(f32[256]{0:T(256)} %param.12) | copy-start | bytes 3076
  170.1 35.0 %copy-start.3 = (f32[256]{0:T(256)S(1)}, f32[256]{0:T(256)}, u32[]{:S(2)}) copy-start(f32[256]{0:T(256)} %param.13) | copy-start | bytes 3076
  204.5 48.4 %copy-start.1 = (s32[16,512]{1,0:T(8,128)S(1)}, s32[16,512]{1,0:T(8,128)}, u32[]{:S(2)}) copy-start(s32[16,512]{1,0:T(8,128)} %param.15) | copy-start | bytes 98308
  204.6 48.5 %copy-start.6 = (s32[16,512]{1,0:T(8,128)S(1)}, s32[16,512]{1,0:T(8,128)}, u32[]{:S(2)}) copy-start(s32[16,512]{1,0:T(8,128)} %param.14) | copy-start | bytes 98308
  248.9 18.9 %all-to-all-start.1 = ((bf16[2,1,4,64,1,4,256]{6,5,3,0,4,1,2:T(4,128)(2,1)}), bf16[2,1,4,64,1,4,256]{6,5,3,0,4,1,2:T(4,128)(2,1)S(1)}, u32[]{:S(2)}, u32[]{:S(2)}) async-start(bf16[2,1,4,64,1,4,256]{6,5,3,0,4,1,2:T(4,128)(2,1)} %copy.38), calls=%async_computation.1 | async-start | bytes 2097152 | tf_op jit(solution)/shard_map/all_to_all | solution.py:86
